TPU v7x, 32 devices: a whole 2x2x4 slice. The times are simulated.
32 devices in a mesh: enc: 4 (over y, x), pool: 8 (over z, core).
Axes of the slice: x: 2, y: 2, z: 4, core: 2. Of those that a mesh axis runs over, the one named last changes fastest.
Arguments:
- encoded: bfloat16 [2048, 32, 128], P('pool', 'enc'), may hold values from -6 to 6
- slot_items: int32 [2048], replicated, may hold values from 0 to 2047, as said below
- lengths: int32 [2048], P(('enc', 'pool')), may hold values from 1 to 32
- token_mask: int32 [2048, 32], P(('enc', 'pool')), may hold values 0 or 1
Outputs:
- scores: float32 [2048, 192], P(('enc', 'pool'))
Inputs may be any that keep to these rules, and one draw needn't show every extreme that they name: `slot_items`: each item appears in exactly one slot. The slots d * 64 + p * 8 + j, for j below 8, hold items p * 256 to (p + 1) * 256 - 1, those whose encoder rows lie on pool index p.
All inputs are finite; a program needn't handle non-finite values. No bound on the sum of `token_mask` on one device may be relied on, other than what follows from the above.
Results may differ from a plain program's by a relative error of at most 0.00057.
Values may be sent and summed in bfloat16 or wider, within the bound.
No kernel may reach another device: no remote copies, remote signals or barrier semaphores. Data moves between devices by JAX's collectives and lax.ppermute only.
A program may use at most 64 MiB of HBM per device.

v0:
```python
import jax
import jax.numpy as jnp
from jax import lax
from jax.sharding import PartitionSpec as P


def tile_scores(query, query_bias, other, other_bias):
    tok, query_items, width = query.shape
    other_items = other.shape[1]
    rows = min(32, query_items)
    blocks = query_items // rows
    other_flat = other.reshape(tok * other_items, width)
    other_add = other_bias.astype(jnp.float32)[:, :, None]
    other_valid = other_bias == 0
    turned_all = jnp.transpose(query.reshape(tok, blocks, rows, width), (1, 0, 2, 3))
    adding_all = jnp.transpose(
        query_bias.astype(jnp.float32).reshape(tok, blocks, rows), (1, 0, 2)
    )[..., None]
    kept_all = jnp.transpose((query_bias == 0).reshape(tok, blocks, rows), (1, 0, 2))

    def one_block(operands):
        turned, adding, kept = operands
        flat = turned.reshape(tok * rows, width)
        dots_fore = jnp.einsum("ubh,qh->ubq", other, flat, preferred_element_type=jnp.float32)
        fore = jnp.max(dots_fore + other_add, axis=0).reshape(other_items, tok, rows)
        fore = jnp.sum(jnp.where(kept[None], fore, 0.0), axis=1)
        dots_back = jnp.einsum(
            "trh,ch->trc", turned, other_flat, preferred_element_type=jnp.float32
        )
        back = jnp.max(dots_back + adding, axis=0).reshape(rows, tok, other_items)
        back = jnp.sum(jnp.where(other_valid[None], back, 0.0), axis=1)
        return 0.5 * (fore.T + back)

    result = lax.map(one_block, (turned_all, adding_all, kept_all))
    return result.reshape(query_items, other_items)


def shards(encoded, slot_items, lengths, token_mask):
    n_enc = lax.axis_size("enc")
    n_pool = lax.axis_size("pool")
    owners = n_enc * n_pool
    group = encoded.shape[0]
    toks = encoded.shape[1]
    width = encoded.shape[2]
    items_dev = lengths.shape[0]
    per = items_dev // n_pool
    tok = n_enc * toks
    n_tok = items_dev * tok
    pool_index = lax.axis_index("pool")
    table = slot_items.reshape(owners, n_pool, per)
    mine = lax.dynamic_index_in_dim(table, pool_index, 1, keepdims=False) - pool_index * group
    outgoing = jnp.take(encoded, mine, axis=0, mode="clip")
    outgoing = jnp.transpose(outgoing, (2, 0, 1, 3))
    arrived = lax.all_to_all(outgoing, ("enc", "pool"), split_axis=1, concat_axis=1, tiled=True)
    slotted = arrived.reshape(tok, items_dev, width)
    values = slotted.astype(jnp.float32)
    normed = (values / jnp.sqrt(jnp.sum(values * values, axis=-1, keepdims=True) + 1e-06)).astype(
        jnp.bfloat16
    )
    position = jnp.arange(tok, dtype=jnp.int32)[None, :]
    valid = (position < lengths[:, None]) & ((position == 0) | (token_mask == 1))
    valid_tm = jnp.transpose(valid.reshape(items_dev, n_enc, toks), (2, 1, 0)).reshape(
        tok, items_dev
    )
    bias = jnp.where(valid_tm, 0.0, -4.0).astype(jnp.bfloat16)
    packed = jnp.concatenate([normed.reshape(n_tok, width), bias.reshape(-1, width)], axis=0)
    block = packed[:n_tok].reshape(tok, items_dev, width)
    parity = (pool_index ^ pool_index >> 1 ^ pool_index >> 2) & 1
    is_a = pool_index & 1 == 0

    def par(p):
        return (p ^ p >> 1 ^ p >> 2) & 1

    send_pairs = [(p, p ^ (4 if par(p) else 2)) for p in range(n_pool)]
    back_pairs = [(t, s) for s, t in send_pairs]
    chip_pairs = [(p, p ^ 1) for p in range(n_pool)]
    z_recv = lax.ppermute(packed, "pool", send_pairs)
    c_recv = lax.ppermute(packed, "pool", chip_pairs)

    def unpack(received):
        return (
            received[:n_tok].reshape(tok, items_dev, width),
            received[n_tok:].reshape(tok, items_dev),
        )

    half = items_dev // 2
    c_blk, c_bias = unpack(c_recv)
    query = jnp.where(is_a, block[:, :half], c_blk[:, half:])
    query_bias = jnp.where(is_a, bias[:, :half], c_bias[:, half:])
    other = jnp.where(is_a, c_blk, block)
    other_bias = jnp.where(is_a, c_bias, bias)
    part = tile_scores(query, query_bias, other, other_bias)
    part_recv = lax.ppermute(part, "pool", chip_pairs)
    joined = jnp.where(
        is_a, jnp.concatenate([part, part_recv], axis=0), jnp.concatenate([part_recv, part], axis=0)
    )
    tile0 = jnp.where(is_a, joined, joined.T)
    z_blk, z_bias = unpack(z_recv)
    tile_z = tile_scores(block, bias, z_blk, z_bias)
    tile_back = lax.ppermute(tile_z.T, "pool", back_pairs)
    other_items = tile_z.shape[1]
    ready = lax.optimization_barrier(jnp.concatenate([tile0, tile_z, tile_z], axis=1))
    column = jnp.arange(3 * other_items, dtype=jnp.int32)[None, :] // other_items
    back_here = column == 1 + parity
    return jnp.where(back_here, jnp.tile(tile_back, (1, 3)), ready)


def solution(mesh):
    in_specs = (P("pool", "enc", None), P(), P(("enc", "pool")), P(("enc", "pool"), None))
    out_specs = P(("enc", "pool"), None)
    return jax.shard_map(shards, mesh=mesh, in_specs=in_specs, out_specs=out_specs, check_vma=False)
```

profile of v0, /device:TPU:0, one launch (start us, length us, event | category | flops | bytes accessed | tf_op | source)
XLA Modules:
  0.0 54.5 jit_solution(16466838070889059354)
XLA Ops:
  0.0 0.0 copy-start
  0.0 0.8 %reshape.227 = s32[32,8,8]{2,1,0:T(8,128)S(1)} reshape(s32[2048]{0:T(1024)} %param.7) | data formatting | bytes 16384 | tf_op jit(solution)/shard_map/reshape | solution.py:50
  0.9 0.1 subtract_reduce_fusion
  0.9 0.1 reshape.243
  1.0 0.0 copy-done
  1.1 0.8 %gather_fusion = bf16[256,8,128]{2,1,0:T(8,128)(2,1)S(1)} fusion(bf16[256,8,128]{2,1,0:T(8,128)(2,1)S(1)} %copy-done, s32[1024]{0:T(1024)S(1)} %pad_clamp_fusion), kind=kCustom, calls=%fused_computation | custom fusion | bytes 1049600 | tf_op jit(solution)/shard_map/jit(_take)/gather | solution.py:52
  1.9 0.0 copy-start.1
  1.9 0.0 copy-start.2
  1.9 0.9 %copy.53 = bf16[8,32,8,128]{3,2,0,1:T(8,128)(2,1)} copy(bf16[8,32,8,128]{3,0,2,1:T(8,128)(2,1)S(1)} %bitcast.110) | data formatting | bytes 1048576 | tf_op jit(solution)/shard_map/transpose | solution.py:53
  2.8 7.3 %all-to-all-start = ((bf16[8,32,8,128]{3,2,0,1:T(8,128)(2,1)}), bf16[8,32,8,128]{3,2,0,1:T(8,128)(2,1)S(1)}, u32[]{:S(2)}, u32[]{:S(2)}) async-start(bf16[8,32,8,128]{3,2,0,1:T(8,128)(2,1)} %copy.53), calls=%async_computation | async-start | bytes 1048576 | tf_op jit(solution)/shard_map/all_to_all | solution.py:54
  10.1 0.0 copy-done.1
  10.1 0.0 copy-done.2
  10.1 0.1 fusion.10
  10.2 0.1 convert_element_type.104
  10.3 0.1 reshape.240
  10.4 16.0 %all-to-all-done = bf16[8,32,8,128]{3,2,0,1:T(8,128)(2,1)S(1)} async-done(((bf16[8,32,8,128]{3,2,0,1:T(8,128)(2,1)}), bf16[8,32,8,128]{3,2,0,1:T(8,128)(2,1)S(1)}, u32[]{:S(2)}, u32[]{:S(2)}) %all-to-all-start) | async-done | bytes 524320 | tf_op jit(solution)/shard_map/all_to_all | solution.py:54
  26.4 0.3 multiply_reduce_fusion
  26.8 0.1 sqrt.21
  27.0 0.1 copy_convert_fusion
  27.0 0.3 fusion.3
  27.4 0.1 collective-permute-start.2
  27.5 0.1 eq.68
  27.6 0.1 sqrt.22
  27.7 0.1 collective-permute-start
  27.8 0.1 sqrt.20
  27.9 0.3 fusion.6
  28.3 1.3 %collective-permute-done.2 = bf16[2064,128]{1,0:T(8,128)(2,1)} collective-permute-done((bf16[2064,128]{1,0:T(8,128)(2,1)S(1)}, bf16[2064,128]{1,0:T(8,128)(2,1)}, u32[]{:S(2)}, u32[]{:S(2)}) %collective-permute-start.2) | collective-permute-done | bytes 528416 | tf_op jit(solution)/shard_map/ppermute | solution.py:78
  29.5 0.7 %slice.37 = bf16[16,128]{1,0:T(8,128)(2,1)S(1)} slice(bf16[2064,128]{1,0:T(8,128)(2,1)} %collective-permute-done.2), slice={[2048:2064], [0:128]} | slice | bytes 8192 | tf_op jit(solution)/shard_map/slice | solution.py:83
  30.2 0.1 reshape.230
  30.3 0.1 broadcast_compare_fusion.1
  30.4 0.1 fusion.13
  30.5 1.4 %broadcast_select_fusion = (bf16[2048,128]{1,0:T(8,128)(2,1)S(1)}, bf16[2048,128]{1,0:T(8,128)(2,1)S(1)}) fusion(pred[]{:T(512)S(6)} %eq.71, bf16[2064,128]{1,0:T(8,128)(2,1)} %collective-permute-done.2, f32[2048]{0:T(1024)S(1)} %sqrt.21, f32[8,32,8,128]{3,2,1,0:T(8,128)S(1)} %copy_convert_fusion), kind=kLoop, calls=%fused_computation.27 | loop fusion | flops 786432 | bytes 2629633 | tf_op jit(solution)/shard_map/jit(_where)/select_n | solution.py:90
  31.9 0.2 fusion.7
  32.1 1.3 %add_reduce_fusion.2 = f32[32,2048]{1,0:T(8,128)S(1)} fusion(bf16[32,32,128]{2,1,0:T(8,128)(2,1)S(1)} %fusion.7, f32[32,32]{1,0:T(8,128)S(1)} %fusion.13, bf16[2048,128]{1,0:T(8,128)(2,1)S(1)} %get-tuple-element.143), kind=kOutput, calls=%fused_computation.13 | convolution fusion | flops 540999680 | bytes 1052672 | tf_op jit(solution)/shard_map/while/body/eval_jaxpr/trh,ch->trc/dot_general | solution.py:27
  33.4 1.3 %add_reduce_fusion.3 = f32[64,1024]{1,0:T(8,128)S(1)} fusion(f32[32,64]{1,0:T(8,128)S(1)} %fusion.11, bf16[32,64,128]{2,1,0:T(8,128)(2,1)S(1)} %bitcast.115, bf16[1024,128,1]{1,0,2:T(8,128)(2,1)S(1)} %bitcast.119), kind=kOutput, calls=%fused_computation.14 | convolution fusion | flops 540999680 | bytes 1056768 | tf_op jit(solution)/shard_map/while/body/eval_jaxpr/ubh,qh->ubq/dot_general | solution.py:24
  34.7 0.2 copy.59
  34.9 0.2 reshape.234
  35.1 0.1 select_reduce_fusion.2
  35.2 0.2 select_reduce_fusion.3
  35.4 0.2 collective-permute-start.3
  35.6 7.2 %collective-permute-done = bf16[2064,128]{1,0:T(8,128)(2,1)S(1)} collective-permute-done((bf16[2064,128]{1,0:T(8,128)(2,1)S(1)}, bf16[2064,128]{1,0:T(8,128)(2,1)S(1)}, u32[]{:S(2)}, u32[]{:S(2)}) %collective-permute-start) | collective-permute-done | bytes 528416 | tf_op jit(solution)/shard_map/ppermute | solution.py:77
  42.8 0.1 reshape.237
  42.9 0.1 eq.70
  43.0 6.7 %while.2 = (s32[]{:T(128)}, f32[2,32,64]{2,1,0:T(8,128)S(1)}, pred[2,32,32]{2,1,0:T(8,128)(4,1)S(1)}, bf16[2,32,32,128]{3,2,0,1:T(8,128)(2,1)S(1)}, bf16[32,64,1...) while((s32[]{:T(128)}, f32[2,32,64]{2,1,0:T(8,128)S(1)}, ...), condition=%wide.region_6.7_spmd, body=%wide.region_1.6_spmd.sunk | while | flops 1082261504 | bytes 4285557 | solution.py:34
  43.1 1.3 %add_reduce_fusion.6 = f32[32,2048]{1,0:T(8,128)S(1)} fusion(f32[32,32]{1,0:T(8,128)S(1)} %bitcast.116, bf16[2048,128]{1,0:T(8,128)(2,1)S(1)} %get-tuple-element.230, bf16[1,32,32,128]{3,2,0,1:T(8,128)(2,1)S(1)} %constant_dynamic-slice_fusion.5), kind=kOutput, calls=%fused_computation.1.clone.1 | convolution fusion | flops 540999680 | bytes 1052672 | tf_op jit(solution)/shard_map/while/body/eval_jaxpr/trh,ch->trc/dot_general | solution.py:27
  44.4 0.2 reshape.263
  44.6 0.1 select_reduce_fusion.6
  44.7 1.3 %add_reduce_fusion.7 = f32[1024,64]{0,1:T(8,128)S(1)} fusion(f32[32,64]{1,0:T(8,128)S(1)} %bitcast.128, bf16[1024,128,1]{1,0,2:T(8,128)(2,1)S(1)} %bitcast.108, bf16[32,64,128]{2,1,0:T(8,128)(2,1)S(1)} %bitcast.113), kind=kOutput, calls=%fused_computation.2.clone.1 | convolution fusion | flops 540999680 | bytes 1056768 | tf_op jit(solution)/shard_map/while/body/eval_jaxpr/ubh,qh->ubq/dot_general | solution.py:24
  46.0 0.2 copy.72
  46.2 0.2 select_reduce_fusion.7
  46.5 1.3 %add_reduce_fusion.6 = f32[32,2048]{1,0:T(8,128)S(1)} fusion(f32[32,32]{1,0:T(8,128)S(1)} %bitcast.116, bf16[2048,128]{1,0:T(8,128)(2,1)S(1)} %get-tuple-element.230, bf16[1,32,32,128]{3,2,0,1:T(8,128)(2,1)S(1)} %constant_dynamic-slice_fusion.5), kind=kOutput, calls=%fused_computation.1.clone.1 | convolution fusion | flops 540999680 | bytes 1052672 | tf_op jit(solution)/shard_map/while/body/eval_jaxpr/trh,ch->trc/dot_general | solution.py:27
  47.7 0.2 reshape.263
  48.0 0.1 select_reduce_fusion.6
  48.1 1.3 %add_reduce_fusion.7 = f32[1024,64]{0,1:T(8,128)S(1)} fusion(f32[32,64]{1,0:T(8,128)S(1)} %bitcast.128, bf16[1024,128,1]{1,0,2:T(8,128)(2,1)S(1)} %bitcast.108, bf16[32,64,128]{2,1,0:T(8,128)(2,1)S(1)} %bitcast.113), kind=kOutput, calls=%fused_computation.2.clone.1 | convolution fusion | flops 540999680 | bytes 1056768 | tf_op jit(solution)/shard_map/while/body/eval_jaxpr/ubh,qh->ubq/dot_general | solution.py:24
  49.3 0.2 copy.72
  49.5 0.2 select_reduce_fusion.7
  49.8 0.1 collective-permute-start.1
  49.8 0.0 collective-permute-done.3
  49.9 0.1 copy.60
  50.0 0.1 pad_maximum_fusion.1
  50.1 3.7 %collective-permute-done.1 = f32[64,64]{0,1:T(8,128)S(1)} collective-permute-done((f32[64,64]{0,1:T(8,128)S(1)}, f32[64,64]{0,1:T(8,128)S(1)}, u32[]{:S(2)}, u32[]{:S(2)}) %collective-permute-start.1) | collective-permute-done | bytes 16416 | tf_op jit(solution)/shard_map/ppermute | solution.py:100
  53.8 0.1 copy.61
  53.8 0.6 %broadcast_select_fusion.1 = f32[64,192]{1,0:T(8,128)} fusion(f32[64,192]{1,0:T(8,128)S(1)} %copy.61, f32[64,192]{1,0:T(8,128)S(1)} %pad_maximum_fusion.1, pred[192]{0:T(512)(128)(4,1)S(1)} %fusion.12), kind=kLoop, calls=%fused_computation.33 | loop fusion | flops 12288 | bytes 147648 | tf_op jit(solution)/shard_map/jit(_where)/select_n | solution.py:105
  (26 shorter events, 0.4 us)
Async XLA Ops:
  0.0 1.1 %copy-start = (bf16[256,8,128]{2,1,0:T(8,128)(2,1)S(1)}, bf16[256,8,128]{2,1,0:T(8,128)(2,1)}, u32[]{:S(2)}) copy-start(bf16[256,8,128]{2,1,0:T(8,128)(2,1)} %param.6) | copy-start | bytes 1572868
  1.9 8.2 %copy-start.1 = (s32[64,32]{0,1:T(8,128)S(1)}, s32[64,32]{0,1:T(8,128)}, u32[]{:S(2)}) copy-start(s32[64,32]{0,1:T(8,128)} %param.9) | copy-start | bytes 24580
  1.9 8.2 %copy-start.2 = (s32[64]{0:T(128)S(1)}, s32[64]{0:T(128)}, u32[]{:S(2)}) copy-start(s32[64]{0:T(128)} %param.8) | copy-start | bytes 772
  2.8 23.7 %all-to-all-start = ((bf16[8,32,8,128]{3,2,0,1:T(8,128)(2,1)}), bf16[8,32,8,128]{3,2,0,1:T(8,128)(2,1)S(1)}, u32[]{:S(2)}, u32[]{:S(2)}) async-start(bf16[8,32,8,128]{3,2,0,1:T(8,128)(2,1)} %copy.53), calls=%async_computation | async-start | bytes 1048576 | tf_op jit(solution)/shard_map/all_to_all | solution.py:54
  27.4 2.1 %collective-permute-start.2 = (bf16[2064,128]{1,0:T(8,128)(2,1)S(1)}, bf16[2064,128]{1,0:T(8,128)(2,1)}, u32[]{:S(2)}, u32[]{:S(2)}) collective-permute-start(bf16[2064,128]{1,0:T(8,128)(2,1)S(1)} %pad_maximum_fusion), channel_id=1, source_target_pairs={{0,1},{1,0},{2,3},{3,2},{4,5},{5,4},{6,7},{7,6},{8,9},{9,8},{10,11... | collective-permute-start | bytes 1585160 | tf_op jit(solution)/shard_map/ppermute | solution.py:78
  27.7 15.1 %collective-permute-start = (bf16[2064,128]{1,0:T(8,128)(2,1)S(1)}, bf16[2064,128]{1,0:T(8,128)(2,1)S(1)}, u32[]{:S(2)}, u32[]{:S(2)}) collective-permute-start(bf16[2064,128]{1,0:T(8,128)(2,1)S(1)} %pad_maximum_fusion), channel_id=1, source_target_pairs={{0,2},{1,5},{2,6},{3,1},{4,0},{5,7},{6,4},{7,3},{8,10},{9,13},{10,... | collective-permute-start | bytes 1585160 | tf_op jit(solution)/shard_map/ppermute | solution.py:77
  35.4 14.4 %collective-permute-start.3 = (f32[32,64]{1,0:T(8,128)S(1)}, f32[32,64]{1,0:T(8,128)S(1)}, u32[]{:S(2)}, u32[]{:S(2)}) collective-permute-start(f32[32,64]{1,0:T(8,128)S(1)} %fusion.8), channel_id=1, source_target_pairs={{0,1},{1,0},{2,3},{3,2},{4,5},{5,4},{6,7},{7,6},{8,9},{9,8},{10,11... | collective-permute-start | bytes 24584 | tf_op jit(solution)/shard_map/ppermute | solution.py:93
  49.8 4.0 %collective-permute-start.1 = (f32[64,64]{0,1:T(8,128)S(1)}, f32[64,64]{0,1:T(8,128)S(1)}, u32[]{:S(2)}, u32[]{:S(2)}) collective-permute-start(f32[64,64]{0,1:T(8,128)S(1)} %bitcast.126), channel_id=1, source_target_pairs={{2,0},{5,1},{6,2},{1,3},{0,4},{7,5},{4,6},{3,7},{10,8},{13,9},{14,... | collective-permute-start | bytes 49160 | tf_op jit(solution)/shard_map/ppermute | solution.py:100
where the time goes:
time: 54.8 us; the launch traced here: 54.5 us
  waiting for transfers between devices  28.2 us (51%)
  starting transfers between devices  7.69 us (14%)
  matrix products  7.58 us (14%)
  local copies, waits for them, and re-layouts  5.71 us (10%)
  other arithmetic  4.8 us (9%)
    all_to_all x1, waiting for transfers between devices, shards(): lax.all_to_all(outgoing, ('enc', 'pool'), split_axis=1, concat_axis=1, ti...  16 us
    all_to_all x1, starting transfers between devices, shards(): lax.all_to_all(outgoing, ('enc', 'pool'), split_axis=1, concat_axis=1, ti...  7.3 us
    ppermute x1, waiting for transfers between devices, shards(): z_recv = lax.ppermute(packed, 'pool', send_pairs)  7.19 us
    dot_general x3, matrix products, one_block(): jnp.einsum('ubh,qh->ubq', other, flat, preferred_element_type=jnp.float32)  3.79 us
    dot_general x3, matrix products, one_block(): jnp.einsum('trh,ch->trc', turned, other_flat, preferred_element_type=jnp....  3.79 us
    ppermute x1, waiting for transfers between devices, shards(): tile_back = lax.ppermute(tile_z.T, 'pool', back_pairs)  3.69 us
    select_n x1, other arithmetic, shards(): other = jnp.where(is_a, c_blk, block)  1.4 us
    ppermute x1, waiting for transfers between devices, shards(): c_recv = lax.ppermute(packed, 'pool', chip_pairs)  1.27 us
  transfers between devices with their start and end apart: 5, of which 4 were waited for; matrix products, arithmetic and copies ran while one was open for 25% of the time, Pallas kernels for 0%

commit v1 on v0

--- a/solution.py
+++ b/solution.py
@@ -51,7 +51,15 @@
     mine = lax.dynamic_index_in_dim(table, pool_index, 1, keepdims=False) - pool_index * group
     outgoing = jnp.take(encoded, mine, axis=0, mode="clip")
     outgoing = jnp.transpose(outgoing, (2, 0, 1, 3))
-    arrived = lax.all_to_all(outgoing, ("enc", "pool"), split_axis=1, concat_axis=1, tiled=True)
+    arrived = jnp.concatenate(
+        lax.all_to_all(
+            jnp.stack(jnp.split(outgoing, lax.axis_size(("enc", "pool")), axis=1)),
+            ("enc", "pool"),
+            0,
+            0,
+        ),
+        axis=1,
+    )
     slotted = arrived.reshape(tok, items_dev, width)
     values = slotted.astype(jnp.float32)
     normed = (values / jnp.sqrt(jnp.sum(values * values, axis=-1, keepdims=True) + 1e-06)).astype(

time: 54.8 us -> 73.6 us (1.34)
  local copies, waits for them, and re-layouts: 5.71 us -> 24.4 us
    unnamed x6 -> x37, local copies, waits for them, and re-layouts: 0.04 us -> 18.6 us
    transpose x1 -> x0, local copies, waits for them, and re-layouts: 0.89 us -> none  [shards(): outgoing = jnp.transpose(outgoing, (2, 0, 1, 3))]
  transfers between devices with their start and end apart: 5 -> 5, of which waited for: 4 -> 4; matrix products, arithmetic and copies ran while one was open for 25% -> 19% of each run, Pallas kernels for 0% -> 0%
where the time goes in v1:
time: 73.6 us; the launch traced here: 73.2 us
  waiting for transfers between devices  28.2 us (38%)
  local copies, waits for them, and re-layouts  24.4 us (33%)
  starting transfers between devices  7.7 us (10%)
  matrix products  7.6 us (10%)
  other arithmetic  4.85 us (7%)
    unnamed x37, local copies, waits for them, and re-layouts  18.6 us
    all_to_all x1, waiting for transfers between devices, shards(): lax.all_to_all(jnp.stack(jnp.split(outgoing, lax.axis_size(('enc', 'pool'...  16 us
    all_to_all x1, starting transfers between devices, shards(): lax.all_to_all(jnp.stack(jnp.split(outgoing, lax.axis_size(('enc', 'pool'...  7.3 us
    ppermute x1, waiting for transfers between devices, shards(): z_recv = lax.ppermute(packed, 'pool', send_pairs)  7.18 us
    dot_general x3, matrix products, one_block(): jnp.einsum('trh,ch->trc', turned, other_flat, preferred_element_type=jnp....  3.8 us
    dot_general x3, matrix products, one_block(): jnp.einsum('ubh,qh->ubq', other, flat, preferred_element_type=jnp.float32)  3.8 us
    ppermute x1, waiting for transfers between devices, shards(): tile_back = lax.ppermute(tile_z.T, 'pool', back_pairs)  3.69 us
  transfers between devices with their start and end apart: 5, of which 4 were waited for; matrix products, arithmetic and copies ran while one was open for 19% of the time, Pallas kernels for 0%

profile of v1, /device:TPU:0, one launch (start us, length us, event | category | flops | bytes accessed | tf_op | source)
XLA Modules:
  0.0 73.2 jit_solution(10220680917164848235)
XLA Ops:
  0.0 0.8 %reshape.229 = s32[32,8,8]{2,1,0:T(8,128)S(1)} reshape(s32[2048]{0:T(1024)} %param.7) | data formatting | bytes 16384 | tf_op jit(solution)/shard_map/reshape | solution.py:50
  1.1 0.8 %gather_fusion = bf16[256,8,128]{2,1,0:T(8,128)(2,1)S(1)} fusion(bf16[256,8,128]{2,1,0:T(8,128)(2,1)S(1)} %copy-done, s32[1024]{0:T(1024)S(1)} %pad_clamp_fusion), kind=kCustom, calls=%fused_computation | custom fusion | bytes 1049600 | tf_op jit(solution)/shard_map/jit(_take)/gather | solution.py:52
  1.9 0.6 constant_dynamic-update-slice_fusion.31
  2.5 0.6 constant_dynamic-update-slice_fusion.30
  3.1 0.6 constant_dynamic-update-slice_fusion.29
  3.7 0.6 constant_dynamic-update-slice_fusion.28
  4.3 0.6 constant_dynamic-update-slice_fusion.27
  4.9 0.6 constant_dynamic-update-slice_fusion.26
  5.5 0.6 constant_dynamic-update-slice_fusion.25
  6.1 0.6 constant_dynamic-update-slice_fusion.24
  6.7 0.6 constant_dynamic-update-slice_fusion.23
  7.3 0.6 constant_dynamic-update-slice_fusion.22
  7.9 0.6 constant_dynamic-update-slice_fusion.21
  8.5 0.6 constant_dynamic-update-slice_fusion.20
  9.1 0.6 constant_dynamic-update-slice_fusion.19
  9.7 0.6 constant_dynamic-update-slice_fusion.18
  10.3 0.6 constant_dynamic-update-slice_fusion.17
  10.9 0.6 constant_dynamic-update-slice_fusion.16
  11.5 0.6 constant_dynamic-update-slice_fusion.15
  12.1 0.6 constant_dynamic-update-slice_fusion.14
  12.7 0.6 constant_dynamic-update-slice_fusion.13
  13.3 0.6 constant_dynamic-update-slice_fusion.12
  13.9 0.6 constant_dynamic-update-slice_fusion.11
  14.5 0.6 constant_dynamic-update-slice_fusion.10
  15.1 0.6 constant_dynamic-update-slice_fusion.9
  15.7 0.6 constant_dynamic-update-slice_fusion.8
  16.3 0.6 constant_dynamic-update-slice_fusion.7
  16.9 0.6 constant_dynamic-update-slice_fusion.6
  17.5 0.6 constant_dynamic-update-slice_fusion.5
  18.1 0.6 constant_dynamic-update-slice_fusion.4
  18.7 0.6 constant_dynamic-update-slice_fusion.3
  19.3 0.6 constant_dynamic-update-slice_fusion.2
  19.9 0.6 constant_dynamic-update-slice_fusion.1
  20.5 0.6 constant_dynamic-update-slice_fusion
  21.1 7.3 %all-to-all-start = ((bf16[32,8,1,8,128]{4,1,3,2,0:T(8,128)(2,1)}), bf16[32,8,1,8,128]{4,1,3,2,0:T(8,128)(2,1)S(1)}, u32[]{:S(2)}, u32[]{:S(2)}) async-start(bf16[32,8,1,8,128]{4,1,3,2,0:T(8,128)(2,1)} %constant_dynamic-update-slice_fusion), calls=%async_computation | async-start | bytes 1048576 | tf_op jit(solution)/shard_map/all_to_all | solution.py:55
  28.7 16.0 %all-to-all-done = bf16[32,8,1,8,128]{4,1,3,2,0:T(8,128)(2,1)S(1)} async-done(((bf16[32,8,1,8,128]{4,1,3,2,0:T(8,128)(2,1)}), bf16[32,8,1,8,128]{4,1,3,2,0:T(8,128)(2,1)S(1)}, u32[]{:S(2)}, u32[]{:S(2)}) %all-to-all-start) | async-done | bytes 524320 | tf_op jit(solution)/shard_map/all_to_all | solution.py:55
  44.9 0.2 copy.119
  45.1 0.3 fusion.3
  45.8 0.3 fusion.4
  46.7 0.3 fusion.7
  47.0 1.3 %collective-permute-done.2 = bf16[2064,128]{1,0:T(8,128)(2,1)} collective-permute-done((bf16[2064,128]{1,0:T(8,128)(2,1)S(1)}, bf16[2064,128]{1,0:T(8,128)(2,1)}, u32[]{:S(2)}, u32[]{:S(2)}) %collective-permute-start.2) | collective-permute-done | bytes 528416 | tf_op jit(solution)/shard_map/ppermute | solution.py:86
  48.3 0.7 slice.37
  49.2 1.4 %broadcast_select_fusion = (bf16[2048,128]{1,0:T(8,128)(2,1)S(1)}, bf16[2048,128]{1,0:T(8,128)(2,1)S(1)}) fusion(pred[]{:T(512)S(6)} %eq.71, bf16[2064,128]{1,0:T(8,128)(2,1)} %collective-permute-done.2, f32[2048]{0:T(1024)S(1)} %sqrt.21, f32[8,32,1,8,128]{4,3,1,0,2:T(8,128)S(1)} %copy.119), kind=kLoop, calls=%fused_computation.28 | loop fusion | flops 786432 | bytes 2629633 | tf_op jit(solution)/shard_map/jit(_where)/select_n | solution.py:98
  50.6 0.2 fusion.8
  50.9 1.3 %add_reduce_fusion.2 = f32[32,2048]{1,0:T(8,128)S(1)} fusion(bf16[32,32,128]{2,1,0:T(8,128)(2,1)S(1)} %fusion.8, f32[32,32]{1,0:T(8,128)S(1)} %fusion.14, bf16[2048,128]{1,0:T(8,128)(2,1)S(1)} %get-tuple-element.143), kind=kOutput, calls=%fused_computation.13 | convolution fusion | flops 540999680 | bytes 1052672 | tf_op jit(solution)/shard_map/while/body/eval_jaxpr/trh,ch->trc/dot_general | solution.py:27
  52.1 1.3 %add_reduce_fusion.3 = f32[64,1024]{1,0:T(8,128)S(1)} fusion(f32[32,64]{1,0:T(8,128)S(1)} %fusion.12, bf16[32,64,128]{2,1,0:T(8,128)(2,1)S(1)} %bitcast.278, bf16[1024,128,1]{1,0,2:T(8,128)(2,1)S(1)} %bitcast.282), kind=kOutput, calls=%fused_computation.14 | convolution fusion | flops 540999680 | bytes 1056768 | tf_op jit(solution)/shard_map/while/body/eval_jaxpr/ubh,qh->ubq/dot_general | solution.py:24
  53.4 0.2 copy.129
  53.6 0.2 reshape.236
  53.9 0.2 select_reduce_fusion.3
  54.2 0.2 collective-permute-start.3
  54.4 7.2 %collective-permute-done = bf16[2064,128]{1,0:T(8,128)(2,1)S(1)} collective-permute-done((bf16[2064,128]{1,0:T(8,128)(2,1)S(1)}, bf16[2064,128]{1,0:T(8,128)(2,1)S(1)}, u32[]{:S(2)}, u32[]{:S(2)}) %collective-permute-start) | collective-permute-done | bytes 528416 | tf_op jit(solution)/shard_map/ppermute | solution.py:85
  61.8 6.8 %while.2 = (s32[]{:T(128)}, f32[2,32,64]{2,1,0:T(8,128)S(1)}, pred[2,32,32]{2,1,0:T(8,128)(4,1)S(1)}, bf16[2,32,32,128]{3,2,0,1:T(8,128)(2,1)S(1)}, bf16[32,64,1...) while((s32[]{:T(128)}, f32[2,32,64]{2,1,0:T(8,128)S(1)}, ...), condition=%wide.region_6.7_spmd, body=%wide.region_1.6_spmd.sunk | while | flops 1082261504 | bytes 4285557 | solution.py:34
  61.8 1.3 %add_reduce_fusion.6 = f32[32,2048]{1,0:T(8,128)S(1)} fusion(f32[32,32]{1,0:T(8,128)S(1)} %bitcast.279, bf16[2048,128]{1,0:T(8,128)(2,1)S(1)} %get-tuple-element.230, bf16[1,32,32,128]{3,2,0,1:T(8,128)(2,1)S(1)} %constant_dynamic-slice_fusion.5), kind=kOutput, calls=%fused_computation.1.clone.1 | convolution fusion | flops 540999680 | bytes 1052672 | tf_op jit(solution)/shard_map/while/body/eval_jaxpr/trh,ch->trc/dot_general | solution.py:27
  63.1 0.2 reshape.265
  63.4 1.3 %add_reduce_fusion.7 = f32[1024,64]{0,1:T(8,128)S(1)} fusion(f32[32,64]{1,0:T(8,128)S(1)} %bitcast.291, bf16[1024,128,1]{1,0,2:T(8,128)(2,1)S(1)} %bitcast.240, bf16[32,64,128]{2,1,0:T(8,128)(2,1)S(1)} %bitcast.276), kind=kOutput, calls=%fused_computation.2.clone.1 | convolution fusion | flops 540999680 | bytes 1056768 | tf_op jit(solution)/shard_map/while/body/eval_jaxpr/ubh,qh->ubq/dot_general | solution.py:24
  64.7 0.2 copy.139
  64.9 0.2 select_reduce_fusion.7
  65.2 1.3 %add_reduce_fusion.6 = f32[32,2048]{1,0:T(8,128)S(1)} fusion(f32[32,32]{1,0:T(8,128)S(1)} %bitcast.279, bf16[2048,128]{1,0:T(8,128)(2,1)S(1)} %get-tuple-element.230, bf16[1,32,32,128]{3,2,0,1:T(8,128)(2,1)S(1)} %constant_dynamic-slice_fusion.5), kind=kOutput, calls=%fused_computation.1.clone.1 | convolution fusion | flops 540999680 | bytes 1052672 | tf_op jit(solution)/shard_map/while/body/eval_jaxpr/trh,ch->trc/dot_general | solution.py:27
  66.5 0.2 reshape.265
  66.8 1.3 %add_reduce_fusion.7 = f32[1024,64]{0,1:T(8,128)S(1)} fusion(f32[32,64]{1,0:T(8,128)S(1)} %bitcast.291, bf16[1024,128,1]{1,0,2:T(8,128)(2,1)S(1)} %bitcast.240, bf16[32,64,128]{2,1,0:T(8,128)(2,1)S(1)} %bitcast.276), kind=kOutput, calls=%fused_computation.2.clone.1 | convolution fusion | flops 540999680 | bytes 1056768 | tf_op jit(solution)/shard_map/while/body/eval_jaxpr/ubh,qh->ubq/dot_general | solution.py:24
  68.1 0.2 copy.139
  68.3 0.2 select_reduce_fusion.7
  68.8 3.7 %collective-permute-done.1 = f32[64,64]{0,1:T(8,128)S(1)} collective-permute-done((f32[64,64]{0,1:T(8,128)S(1)}, f32[64,64]{0,1:T(8,128)S(1)}, u32[]{:S(2)}, u32[]{:S(2)}) %collective-permute-start.1) | collective-permute-done | bytes 16416 | tf_op jit(solution)/shard_map/ppermute | solution.py:108
  72.6 0.6 broadcast_select_fusion.1
  (58 shorter events, 2.5 us)
Async XLA Ops:
  0.0 1.1 %copy-start = (bf16[256,8,128]{2,1,0:T(8,128)(2,1)S(1)}, bf16[256,8,128]{2,1,0:T(8,128)(2,1)}, u32[]{:S(2)}) copy-start(bf16[256,8,128]{2,1,0:T(8,128)(2,1)} %param.6) | copy-start | bytes 1572868
  1.9 26.6 %copy-start.1 = (s32[64,32]{0,1:T(8,128)S(1)}, s32[64,32]{0,1:T(8,128)}, u32[]{:S(2)}) copy-start(s32[64,32]{0,1:T(8,128)} %param.9) | copy-start | bytes 24580
  1.9 26.6 %copy-start.2 = (s32[64]{0:T(128)S(1)}, s32[64]{0:T(128)}, u32[]{:S(2)}) copy-start(s32[64]{0:T(128)} %param.8) | copy-start | bytes 772
  21.1 23.7 %all-to-all-start = ((bf16[32,8,1,8,128]{4,1,3,2,0:T(8,128)(2,1)}), bf16[32,8,1,8,128]{4,1,3,2,0:T(8,128)(2,1)S(1)}, u32[]{:S(2)}, u32[]{:S(2)}) async-start(bf16[32,8,1,8,128]{4,1,3,2,0:T(8,128)(2,1)} %constant_dynamic-update-slice_fusion), calls=%async_computation | async-start | bytes 1048576 | tf_op jit(solution)/shard_map/all_to_all | solution.py:55
  46.2 2.1 %collective-permute-start.2 = (bf16[2064,128]{1,0:T(8,128)(2,1)S(1)}, bf16[2064,128]{1,0:T(8,128)(2,1)}, u32[]{:S(2)}, u32[]{:S(2)}) collective-permute-start(bf16[2064,128]{1,0:T(8,128)(2,1)S(1)} %pad_maximum_fusion), channel_id=1, source_target_pairs={{0,1},{1,0},{2,3},{3,2},{4,5},{5,4},{6,7},{7,6},{8,9},{9,8},{10,11... | collective-permute-start | bytes 1585160 | tf_op jit(solution)/shard_map/ppermute | solution.py:86
  46.5 15.1 %collective-permute-start = (bf16[2064,128]{1,0:T(8,128)(2,1)S(1)}, bf16[2064,128]{1,0:T(8,128)(2,1)S(1)}, u32[]{:S(2)}, u32[]{:S(2)}) collective-permute-start(bf16[2064,128]{1,0:T(8,128)(2,1)S(1)} %pad_maximum_fusion), channel_id=1, source_target_pairs={{0,2},{1,5},{2,6},{3,1},{4,0},{5,7},{6,4},{7,3},{8,10},{9,13},{10,... | collective-permute-start | bytes 1585160 | tf_op jit(solution)/shard_map/ppermute | solution.py:85
  54.2 14.4 %collective-permute-start.3 = (f32[32,64]{1,0:T(8,128)S(1)}, f32[32,64]{1,0:T(8,128)S(1)}, u32[]{:S(2)}, u32[]{:S(2)}) collective-permute-start(f32[32,64]{1,0:T(8,128)S(1)} %fusion.9), channel_id=1, source_target_pairs={{0,1},{1,0},{2,3},{3,2},{4,5},{5,4},{6,7},{7,6},{8,9},{9,8},{10,11... | collective-permute-start | bytes 24584 | tf_op jit(solution)/shard_map/ppermute | solution.py:101
  68.5 4.0 %collective-permute-start.1 = (f32[64,64]{0,1:T(8,128)S(1)}, f32[64,64]{0,1:T(8,128)S(1)}, u32[]{:S(2)}, u32[]{:S(2)}) collective-permute-start(f32[64,64]{0,1:T(8,128)S(1)} %bitcast.289), channel_id=1, source_target_pairs={{2,0},{5,1},{6,2},{1,3},{0,4},{7,5},{4,6},{3,7},{10,8},{13,9},{14,... | collective-permute-start | bytes 49160 | tf_op jit(solution)/shard_map/ppermute | solution.py:108
